TPU v7x, 32 devices: a whole 2x2x4 slice. The times are simulated.
32 devices in a mesh: dp: 8 (over z, core), tensor: 4 (over y, x).
Axes of the slice: x: 2, y: 2, z: 4, core: 2. Of those that a mesh axis runs over, the one named last changes fastest.
Arguments:
- t_index: int32 [8], P('dp'), may hold values from 0 to 999
- cond_slot: int32 [8], P('dp'), may hold values from 0 to 1
- positions: int32 [8, 3, 512], P('dp'), may hold values from 0 to 63, as said below
- latent: bfloat16 [8, 512, 5120], P('dp', 'tensor'), may hold values from -6 to 6
- teacher_query: bfloat16 [2, 8, 512, 4096], P(None, 'dp', None, 'tensor'), may hold values from -6 to 6
- teacher_key: bfloat16 [2, 8, 512, 4096], P(None, 'dp', None, 'tensor'), may hold values from -6 to 6
- teacher_value: bfloat16 [2, 8, 512, 4096], P(None, 'dp', None, 'tensor'), may hold values from -6 to 6
- student_query: bfloat16 [8, 512, 4096], P('dp', 'tensor'), may hold values from -6 to 6
- student_key: bfloat16 [8, 512, 4096], P('dp', 'tensor'), may hold values from -6 to 6
- student_value: bfloat16 [8, 512, 4096], P('dp', 'tensor'), may hold values from -6 to 6
- query_tangent: bfloat16 [8, 512, 4096], P('dp', 'tensor'), may hold values from -6 to 6
- key_tangent: bfloat16 [8, 512, 4096], P('dp', 'tensor'), may hold values from -6 to 6
- value_tangent: bfloat16 [8, 512, 4096], P('dp', 'tensor'), may hold values from -6 to 6
- teacher_out: bfloat16 [4096, 5120], P('tensor', 'dp'), may hold values from -0.375 to 0.375
- student_out: bfloat16 [4096, 5120], P('tensor', 'dp'), may hold values from -0.375 to 0.375
Outputs:
- target: bfloat16 [8, 512, 5120], P('dp', 'tensor')
- gradient: float32 [4096, 5120], P('tensor', 'dp')
Inputs may be any that keep to these rules, and one draw needn't show every extreme that they name: `positions`: within each clip, tokens 64 m and 64 m + 1 have equal coordinates on all three axes.
All inputs are finite; a program needn't handle non-finite values.
Results may differ from a plain program's by a relative error of at most 0.015.
Values may be sent and summed in bfloat16 or wider, within the bound.
No kernel may reach another device: no remote copies, remote signals or barrier semaphores. Data moves between devices by JAX's collectives and lax.ppermute only.
A program may use at most 192 MiB of HBM per device.

v0:
```python
import math
import jax
import jax.numpy as jnp
from jax import lax
from jax.sharding import PartitionSpec as P

HD = 128
STEPS = 1000
sigma_data = 0.5
guidance = 5.0


def rope_angles(coords):
    half_size = HD // 2
    sixth = HD // 6
    first_pairs = half_size - 2 * sixth
    pair_index = jnp.arange(half_size)
    axis_id = (pair_index >= first_pairs).astype(jnp.int32) + (
        pair_index >= first_pairs + sixth
    ).astype(jnp.int32)
    offset = jnp.where(axis_id == 0, 0, jnp.where(axis_id == 1, first_pairs, first_pairs + sixth))
    axis_width = jnp.where(axis_id == 0, 2 * first_pairs, 2 * sixth)
    exponent = 2.0 * (pair_index - offset).astype(jnp.float32) / axis_width.astype(jnp.float32)
    frequency = jnp.exp(-exponent * math.log(10000.0))
    angles = jnp.zeros((coords.shape[1], half_size), jnp.float32)
    for which_axis in range(3):
        chosen = jnp.where(axis_id == which_axis, frequency, 0.0)
        angles = angles + coords[which_axis].astype(jnp.float32)[:, None] * chosen[None, :]
    return angles


def rotate_heads(source, angles):
    half_size = source.shape[-1] // 2
    cos_angle = jnp.cos(angles)[:, None, :]
    sin_angle = jnp.sin(angles)[:, None, :]
    front_half = source[..., :half_size]
    back_half = source[..., half_size:]
    return jnp.concatenate(
        [
            front_half * cos_angle - back_half * sin_angle,
            back_half * cos_angle + front_half * sin_angle,
        ],
        axis=-1,
    )


def split_heads(source):
    return source.reshape(source.shape[0], -1, HD)


def rotated(source, angles):
    row_count = source.shape[0]
    return (
        rotate_heads(split_heads(source).astype(jnp.float32), angles)
        .astype(jnp.bfloat16)
        .reshape(row_count, -1)
    )


def softmax_rows(scores):
    row_peak = jnp.max(scores, axis=-1, keepdims=True)
    exponent = jnp.exp(scores - row_peak)
    return exponent / jnp.sum(exponent, axis=-1, keepdims=True)


def attend_plain(queries, key_rows, value_rows):
    scores = jnp.einsum(
        "qhd,khd->hqk", queries, key_rows, preferred_element_type=jnp.float32
    ) * HD ** (-0.5)
    rounded = softmax_rows(scores).astype(jnp.bfloat16)
    return jnp.einsum("hqk,khd->qhd", rounded, value_rows, preferred_element_type=jnp.float32)


def attend_tangent(queries, key_rows, value_rows, query_dir, key_dir, value_dir):
    score_scale = HD ** (-0.5)
    scores = (
        jnp.einsum("qhd,khd->hqk", queries, key_rows, preferred_element_type=jnp.float32)
        * score_scale
    )
    weights = softmax_rows(scores)
    rounded = weights.astype(jnp.bfloat16)
    primal = jnp.einsum("hqk,khd->qhd", rounded, value_rows, preferred_element_type=jnp.float32)
    score_dir = (
        jnp.einsum("qhd,khd->hqk", query_dir, key_rows, preferred_element_type=jnp.float32)
        + jnp.einsum("qhd,khd->hqk", queries, key_dir, preferred_element_type=jnp.float32)
    ) * score_scale
    weight_dir = weights * (score_dir - jnp.sum(weights * score_dir, axis=-1, keepdims=True))
    rounded_dir = weight_dir.astype(jnp.bfloat16)
    tangent = jnp.einsum(
        "hqk,khd->qhd", rounded_dir, value_rows, preferred_element_type=jnp.float32
    ) + jnp.einsum("hqk,khd->qhd", rounded, value_dir, preferred_element_type=jnp.float32)
    return (primal, tangent)


def local(
    t_index,
    cond_slot,
    positions,
    latent,
    teacher_query,
    teacher_key,
    teacher_value,
    student_query,
    student_key,
    student_value,
    query_tangent,
    key_tangent,
    value_tangent,
    teacher_out,
    student_out,
):
    groups = lax.axis_size("tensor")
    seq_local = latent.shape[1]
    seq_whole = seq_local * groups
    row_start = lax.axis_index("tensor") * seq_local
    time_value = 0.2 + 1.2 * (t_index[0].astype(jnp.float32) + 0.5) / STEPS
    cos_time = jnp.cos(time_value)
    sin_time = jnp.sin(time_value)
    angles_whole = rope_angles(positions[0])
    angles_local = lax.dynamic_slice_in_dim(angles_whole, row_start, seq_local, 0)
    outgoing = (
        rotated(student_query[0], angles_local),
        rotated(student_key[0], angles_local),
        student_value[0],
        rotated(query_tangent[0], angles_local),
        rotated(key_tangent[0], angles_local),
        value_tangent[0],
    )
    arrived = (
        lax.all_to_all(outgoing[0], "tensor", split_axis=1, concat_axis=0, tiled=True),
        lax.all_to_all(outgoing[1], "tensor", split_axis=1, concat_axis=0, tiled=True),
        lax.all_to_all(outgoing[2], "tensor", split_axis=1, concat_axis=0, tiled=True),
        lax.all_to_all(outgoing[3], "tensor", split_axis=1, concat_axis=0, tiled=True),
        lax.all_to_all(outgoing[4], "tensor", split_axis=1, concat_axis=0, tiled=True),
        lax.all_to_all(outgoing[5], "tensor", split_axis=1, concat_axis=0, tiled=True),
    )
    outputs = []
    for stream in range(2):
        outputs.append(
            attend_plain(
                split_heads(rotated(teacher_query[stream, 0], angles_whole)),
                split_heads(rotated(teacher_key[stream, 0], angles_whole)),
                split_heads(teacher_value[stream, 0]),
            )
        )
    cond_index = cond_slot[0]
    cond_out = jnp.where(cond_index == 0, outputs[0], outputs[1])
    uncond_out = jnp.where(cond_index == 0, outputs[1], outputs[0])
    teacher_term = (
        (cos_time * cos_time * sigma_data * (uncond_out + guidance * (cond_out - uncond_out)))
        .astype(jnp.bfloat16)
        .reshape(seq_whole, -1)
    )
    primal, tangent = attend_tangent(
        split_heads(arrived[0]),
        split_heads(arrived[1]),
        split_heads(arrived[2]),
        split_heads(arrived[3]),
        split_heads(arrived[4]),
        split_heads(arrived[5]),
    )
    student_term = (
        (-(cos_time * cos_time) * sigma_data * primal - cos_time * sin_time * sigma_data * tangent)
        .astype(jnp.bfloat16)
        .reshape(seq_whole, -1)
    )
    attended = primal.astype(jnp.bfloat16).reshape(seq_whole, -1)
    stacked = jnp.stack([student_out, teacher_out])
    pieces = lax.all_gather(stacked, "dp", axis=2, tiled=True)
    partial_value = jnp.dot(student_term, pieces[0], preferred_element_type=jnp.float32) + jnp.dot(
        teacher_term, pieces[1], preferred_element_type=jnp.float32
    )
    latent_weight = cos_time * sin_time
    clips = lax.axis_size("dp")
    copies = jnp.broadcast_to(attended[None], (clips,) + attended.shape)
    attended_all = lax.all_to_all(copies, "dp", split_axis=0, concat_axis=0, tiled=True)
    velocity = lax.psum_scatter(
        partial_value.astype(jnp.bfloat16), "tensor", scatter_dimension=0, tiled=True
    )
    velocity, attended_all = lax.optimization_barrier((velocity, attended_all))
    target = (velocity.astype(jnp.float32) - latent_weight * latent[0].astype(jnp.float32)).astype(
        jnp.bfloat16
    )
    width = target.shape[1] // clips
    columns = lax.all_to_all(
        target.reshape(seq_local, clips, width), "dp", split_axis=1, concat_axis=1, tiled=True
    )
    columns = lax.all_gather(columns, "tensor", axis=0, tiled=True)
    grad_scale = -2.0 / math.sqrt(clips * seq_whole)
    terms = jnp.einsum("csi,scd->cid", attended_all, columns, preferred_element_type=jnp.float32)
    gradient = jnp.sum((grad_scale * terms).astype(jnp.bfloat16).astype(jnp.float32), axis=0)
    return (target[None], gradient)


def solution(mesh):
    placed = (
        P("dp"),
        P("dp"),
        P("dp", None, None),
        P("dp", "tensor", None),
        P(None, "dp", None, "tensor"),
        P(None, "dp", None, "tensor"),
        P(None, "dp", None, "tensor"),
        P("dp", "tensor", None),
        P("dp", "tensor", None),
        P("dp", "tensor", None),
        P("dp", "tensor", None),
        P("dp", "tensor", None),
        P("dp", "tensor", None),
        P("tensor", "dp"),
        P("tensor", "dp"),
    )
    return jax.shard_map(
        local,
        mesh=mesh,
        in_specs=placed,
        out_specs=(P("dp", "tensor", None), P("tensor", "dp")),
        check_vma=False,
    )
```

profile of v0, /device:TPU:0, one launch (start us, length us, event | category | flops | bytes accessed | tf_op | source)
XLA Modules:
  0.0 523.6 jit_solution(12055977299198744937)
XLA Ops:
  7.2 3.6 pad_maximum_fusion
  11.4 2.6 copy.142
  14.0 2.6 copy.146
  16.6 1.6 copy.135
  19.1 6.6 %subtract_convert_fusion.5 = (bf16[128,32,64]{0,2,1:T(8,128)(2,1)}, bf16[128,32,64]{0,2,1:T(8,128)(2,1)}, bf16[128,32,64]{0,2,1:T(8,128)(2,1)}, bf16[128,32,64]{...) fusion(f32[128,32,128]{0,2,1:T(8,128)} %bitcast.104, ...), kind=kLoop, calls=%fused_computation.76 | loop fusion | flops 8388608 | bytes 12648448 | tf_op jit(solution)/shard_map/convert.16
  26.7 5.3 %all-to-all-start = ((bf16[128,4,1024]{0,2,1:T(8,128)(2,1)}), bf16[128,4,1024]{0,2,1:T(8,128)(2,1)}, u32[]{:S(2)}, u32[]{:S(2)}) async-start(bf16[128,4,1024]{0,2,1:T(8,128)(2,1)} %bitcast.5), calls=%async_computation | async-start | bytes 2097152 | tf_op jit(solution)/shard_map/all_to_all | solution.py:130
  32.9 2.7 fusion.91
  36.2 1.7 fusion.96
  37.8 1.8 copy.179
  39.7 3.2 copy.180
  42.9 3.1 fusion.90
  46.0 1.5 copy.181
  47.5 1.6 fusion.95
  49.1 3.2 copy.182
  52.3 3.2 copy.183
  55.6 1.5 copy.184
  57.1 1.6 fusion.94
  58.7 3.1 copy.185
  61.8 3.2 copy.186
  65.0 1.5 copy.187
  66.5 1.6 fusion.93
  68.1 3.2 copy.188
  71.4 3.2 copy.189
  74.6 2.3 pad_maximum_fusion.2
  77.9 4.2 all-to-all-start.1
  82.2 8.8 %subtract_convert_fusion = (bf16[512,8,64]{2,0,1:T(8,128)(2,1)S(1)}, bf16[512,8,64]{2,0,1:T(8,128)(2,1)}, bf16[512,8,64]{2,0,1:T(8,128)(2,1)}, bf16[512,8,64]{2,...) fusion(f32[512,8,64]{2,0,1:T(8,128)} %copy.189, ...), kind=kLoop, calls=%fused_computation.41 | loop fusion | flops 8388608 | bytes 12845056 | tf_op jit(solution)/shard_map/convert.8
  90.9 5.4 %all-to-all-done.1 = bf16[128,4,1024]{0,2,1:T(8,128)(2,1)} async-done(((bf16[128,4,1024]{0,2,1:T(8,128)(2,1)}), bf16[128,4,1024]{0,2,1:T(8,128)(2,1)}, u32[]{:S(2)}, u32[]{:S(2)}) %all-to-all-start.1) | async-done | bytes 1048608 | tf_op jit(solution)/shard_map/all_to_all | solution.py:131
  96.3 4.8 all-to-all-start.3
  101.1 7.0 %fusion.30 = f32[8,512,512]{1,2,0:T(8,128)} fusion(bf16[512,8,64]{2,0,1:T(8,128)(2,1)} %get-tuple-element.40, bf16[512,8,64]{2,0,1:T(8,128)(2,1)} %get-tuple-element.41, bf16[512,8,64]{2,0,1:T(8,128)(2,1)} %get-tuple-element.36, bf16[512,8,64]{2,0,1:T(8,128)(2,1)} %get-tuple-element.37), kind=kOutput, calls=%fused_computation.58 | convolution fusion | flops 541065216 | bytes 10485760 | tf_op jit(solution)/shard_map/qhd,khd->hqk/dot_general | solution.py:67
  110.6 8.0 %fusion.97 = f32[8,512]{1,0:T(8,128)S(1)} fusion(f32[8,512,512]{1,2,0:T(8,128)} %fusion.30), kind=kOutput, calls=%fused_computation.125 | output fusion | flops 8389119 | bytes 8404992 | tf_op jit(solution)/shard_map/sub | solution.py:62
  118.6 4.3 all-to-all-start.4
  122.9 2.6 fusion.37
  125.5 3.3 copy-done.1
  128.9 2.2 fusion.98
  131.1 5.0 all-to-all-done.4
  136.1 4.4 all-to-all-start.2
  140.5 1.7 fusion.92
  146.1 10.2 %fusion.19 = f32[8,512,128]{1,2,0:T(8,128)} fusion(bf16[512,8,128]{0,2,1:T(8,128)(2,1)S(1)} %bitcast.125, f32[8,512]{1,0:T(8,128)S(1)} %fusion.97, f32[8,512,512]{1,2,0:T(8,128)} %fusion.30), kind=kOutput, calls=%fused_computation.30 | convolution fusion | flops 547361280 | bytes 11550720 | tf_op jit(solution)/shard_map/hqk,khd->qhd/dot_general | solution.py:71
  156.3 10.8 %fusion.25 = bf16[512,8,128]{0,2,1:T(8,128)(2,1)} fusion(f32[8,512,128]{1,2,0:T(8,128)} %fusion.19, f32[]{:T(128)} %bitcast.26, pred[]{:T(512)} %bitcast.27, bf16[512,8,128]{0,2,1:T(8,128)(2,1)S(1)} %bitcast.124, f32[8,512]{1,0:T(8,128)S(1)} %fusion.98, f32[8,512,512]{1,2,0:T(8,128)} %copy-done.1), kind=kOutput, calls=%fused_computation.39 | convolution fusion | flops 551031296 | bytes 12599301 | tf_op jit(solution)/shard_map/hqk,khd->qhd/dot_general | solution.py:71
  167.1 1.5 copy.134
  168.9 1.5 copy.136
  170.7 2.3 copy.143
  172.9 1.5 copy.193
  174.4 2.3 copy.147
  176.7 2.5 copy.194
  179.2 4.5 all-to-all-start.5
  183.7 3.1 copy.140
  186.7 2.3 reshape.307
  190.3 5.0 fusion.99
  196.2 10.9 %fusion.100 = (bf16[8,512,128]{1,2,0:T(8,128)(2,1)}, f32[8,512,128]{1,2,0:T(8,128)}) fusion(bf16[512,8,128]{0,2,1:T(8,128)(2,1)} %reshape.307, f32[8,512]{1,0:T(8,128)S(1)} %get-tuple-element.56, f32[8,512,512]{1,2,0:T(8,128)} %copy-done), kind=kOutput, calls=%fused_computation.128 | convolution fusion | flops 547885568 | bytes 12599296 | tf_op jit(solution)/shard_map/hqk,khd->qhd/dot_general | solution.py:82
  207.1 4.5 fusion.45
  211.6 5.3 %broadcast_in_dim.28 = bf16[8,512,1024]{1,2,0:T(8,128)(2,1)} broadcast(bf16[512,1024]{0,1:T(8,128)(2,1)} %bitcast.122), dimensions={1,2} | broadcast | bytes 9437184 | tf_op jit(solution)/shard_map/broadcast_in_dim | solution.py:175
  216.9 5.1 all-to-all-start.6
  222.1 10.0 %multiply_reduce_fusion = (f32[8,512]{1,0:T(8,128)S(1)}, f32[8,512,512]{1,2,0:T(8,128)}) fusion(f32[8,512,512]{1,2,0:T(8,128)} %get-tuple-element.57, f32[8,512]{1,0:T(8,128)S(1)} %get-tuple-element.56, f32[8,512,512]{1,2,0:T(8,128)} %fusion.45, bf16[512,8,128]{2,1,0:T(8,128)(2,1)S(1)} %bitcast.123, bf16[512,8,128]{2,1,0:T(8,128)(2,1)S(1)} %bitcast.110), kind=kOutput, calls=%fused_computation.15 | convolution fusion | flops 547352576 | bytes 27295744 | tf_op jit(solution)/shard_map/qhd,khd->hqk/dot_general | solution.py:85
  232.1 2.0 copy.152
  234.6 10.2 %fusion.28 = f32[8,512,128]{1,2,0:T(8,128)} fusion(bf16[512,8,128]{0,2,1:T(8,128)(2,1)S(1)} %reshape.310, f32[8,512]{1,0:T(8,128)S(1)} %get-tuple-element.56, f32[8,512,512]{1,2,0:T(8,128)} %copy-done), kind=kOutput, calls=%fused_computation.51 | convolution fusion | flops 547361280 | bytes 11550720 | tf_op jit(solution)/shard_map/hqk,khd->qhd/dot_general | solution.py:91
  244.9 11.5 %subtract_convert_fusion.4 = bf16[8,512,128]{1,2,0:T(8,128)(2,1)S(1)} fusion(f32[8,512,128]{1,2,0:T(8,128)} %fusion.28, f32[8,512,128]{1,2,0:T(8,128)} %get-tuple-element.61, bf16[512,8,128]{0,2,1:T(8,128)(2,1)S(1)} %copy-done.16, f32[8,512,512]{1,2,0:T(8,128)} %get-tuple-element.59, f32[8,512]{1,0:T(8,128)S(1)} %get-tuple-element.58, f32[]{:T(128)S(6)} %mul.409, ...), kind=kOutput, calls=%fused_computation.48 | convolution fusion | flops 554177024 | bytes 23101448 | tf_op jit(solution)/shard_map/hqk,khd->qhd/dot_general | solution.py:89
  256.5 8.4 %fusion.3 = f32[512,5120]{1,0:T(8,128)S(1)} fusion(bf16[512,1024]{0,1:T(8,128)(2,1)S(1)} %bitcast.119, bf16[2,1024,5120]{2,1,0:T(8,128)(2,1)} %all-gather.3.cloned.1.call-done), kind=kOutput, calls=%fused_computation.6 | convolution fusion | flops 5368709120 | bytes 22020096 | tf_op jit(solution)/shard_map/dot_general | solution.py:170
  264.8 12.0 %add_convert_fusion = bf16[512,5120]{1,0:T(8,128)(2,1)} fusion(f32[512,5120]{1,0:T(8,128)S(1)} %fusion.3, bf16[512,1024]{0,1:T(8,128)(2,1)S(1)} %bitcast.126, bf16[2,1024,5120]{2,1,0:T(8,128)(2,1)} %all-gather.3.cloned.1.call-done), kind=kOutput, calls=%fused_computation.9 | convolution fusion | flops 5373952000 | bytes 27262976 | tf_op jit(solution)/shard_map/dot_general | solution.py:170
  277.2 128.8 %all-to-all-done.6 = bf16[8,512,1024]{1,2,0:T(8,128)(2,1)} async-done(((bf16[8,512,1024]{1,2,0:T(8,128)(2,1)}), bf16[8,512,1024]{1,2,0:T(8,128)(2,1)}, u32[]{:S(2)}, u32[]{:S(2)}) %all-to-all-start.6) | async-done | bytes 8388640 | tf_op jit(solution)/shard_map/all_to_all | solution.py:176
  406.0 1.7 fusion.21
  407.8 35.4 %all_to_all.94 = bf16[128,8,640]{2,0,1:T(8,128)(2,1)} all-to-all(bf16[128,8,640]{2,0,1:T(8,128)(2,1)S(1)} %bitcast.108), channel_id=1, replica_groups=mesh['dp'=8,'tensor'=4] {'dp'}, dimensions={1} | all-to-all | bytes 2621440 | tf_op jit(solution)/shard_map/all_to_all | solution.py:185
  443.2 61.0 %all-gather.5.cloned.1.call-done = bf16[512,8,640]{2,0,1:T(8,128)(2,1)} async-done(((bf16[128,8,640]{2,0,1:T(8,128)(2,1)}), bf16[512,8,640]{2,0,1:T(8,128)(2,1)}) %all-gather.5.cloned.1.call-update) | async-done | bytes 5242896 | tf_op jit(solution)/shard_map/all_gather | solution.py:188
  504.2 12.3 %convert_reduce_fusion = f32[1024,640]{1,0:T(8,128)} fusion(bf16[8,512,1024]{1,2,0:T(8,128)(2,1)} %all-to-all-done.6, bf16[512,8,640]{2,0,1:T(8,128)(2,1)} %all-gather.5.cloned.1.call-done), kind=kOutput, calls=%fused_computation.3 | convolution fusion | flops 5389025280 | bytes 16252928 | tf_op jit(solution)/shard_map/csi,scd->cid/dot_general | solution.py:190
  (68 shorter events, 13.6 us)
Async XLA Ops:
  7.2 3.6 copy-start.11
  7.2 249.3 %all-gather.3.cloned.1.call-start = ((), (), s32[]{:S(2)}) async-start(), calls=%async_computation.9 | async-start | bytes 23592960 | tf_op jit(solution)/shard_map/all_gather | solution.py:169
  11.3 5.3 %copy-start.12 = (bf16[1,128,4096]{2,1,0:T(8,128)(2,1)S(1)}, bf16[1,128,4096]{2,1,0:T(8,128)(2,1)}, u32[]{:S(2)}) copy-start(bf16[1,128,4096]{2,1,0:T(8,128)(2,1)} %param.23) | copy-start | bytes 3145732
  11.4 7.0 %copy-start.17 = (s32[1,3,512]{2,0,1:T(1,128)S(1)}, s32[1,3,512]{2,0,1:T(1,128)}, u32[]{:S(2)}) copy-start(s32[1,3,512]{2,0,1:T(1,128)} %param.17) | copy-start | bytes 18436
  26.7 51.2 %all-to-all-start = ((bf16[128,4,1024]{0,2,1:T(8,128)(2,1)}), bf16[128,4,1024]{0,2,1:T(8,128)(2,1)}, u32[]{:S(2)}, u32[]{:S(2)}) async-start(bf16[128,4,1024]{0,2,1:T(8,128)(2,1)} %bitcast.5), calls=%async_computation | async-start | bytes 2097152 | tf_op jit(solution)/shard_map/all_to_all | solution.py:130
  68.1 8.7 %copy-start.7 = (bf16[128,32,64]{0,2,1:T(8,128)(2,1)S(1)}, bf16[128,32,64]{0,2,1:T(8,128)(2,1)}, u32[]{:S(2)}) copy-start(bf16[128,32,64]{0,2,1:T(8,128)(2,1)} %get-tuple-element.46) | copy-start | bytes 1572868
  68.1 8.7 %copy-start.8 = (bf16[128,32,64]{0,2,1:T(8,128)(2,1)S(1)}, bf16[128,32,64]{0,2,1:T(8,128)(2,1)}, u32[]{:S(2)}) copy-start(bf16[128,32,64]{0,2,1:T(8,128)(2,1)} %get-tuple-element.47) | copy-start | bytes 1572868
  77.9 18.4 %all-to-all-start.1 = ((bf16[128,4,1024]{0,2,1:T(8,128)(2,1)}), bf16[128,4,1024]{0,2,1:T(8,128)(2,1)}, u32[]{:S(2)}, u32[]{:S(2)}) async-start(bf16[128,4,1024]{0,2,1:T(8,128)(2,1)} %bitcast.8), calls=%async_computation.1 | async-start | bytes 2097152 | tf_op jit(solution)/shard_map/all_to_all | solution.py:131
  96.3 22.3 %all-to-all-start.3 = ((bf16[128,4,1024]{0,2,1:T(8,128)(2,1)}), bf16[128,4,1024]{0,2,1:T(8,128)(2,1)}, u32[]{:S(2)}, u32[]{:S(2)}) async-start(bf16[128,4,1024]{0,2,1:T(8,128)(2,1)} %bitcast.113), calls=%async_computation.3 | async-start | bytes 2097152 | tf_op jit(solution)/shard_map/all_to_all | solution.py:133
  101.1 7.1 %copy-start.13 = (bf16[1,128,4096]{2,1,0:T(8,128)(2,1)S(1)}, bf16[1,128,4096]{2,1,0:T(8,128)(2,1)}, u32[]{:S(2)}) copy-start(bf16[1,128,4096]{2,1,0:T(8,128)(2,1)} %param.24) | copy-start | bytes 3145732
  101.1 8.4 %copy-start.5 = (bf16[128,32,64]{0,2,1:T(8,128)(2,1)S(1)}, bf16[128,32,64]{0,2,1:T(8,128)(2,1)}, u32[]{:S(2)}) copy-start(bf16[128,32,64]{0,2,1:T(8,128)(2,1)} %get-tuple-element.14) | copy-start | bytes 1572868
  101.1 8.4 %copy-start.6 = (bf16[128,32,64]{0,2,1:T(8,128)(2,1)S(1)}, bf16[128,32,64]{0,2,1:T(8,128)(2,1)}, u32[]{:S(2)}) copy-start(bf16[128,32,64]{0,2,1:T(8,128)(2,1)} %get-tuple-element.15) | copy-start | bytes 1572868
  110.6 12.3 %copy-start.3 = (bf16[512,8,64]{2,0,1:T(8,128)(2,1)S(1)}, bf16[512,8,64]{2,0,1:T(8,128)(2,1)}, u32[]{:S(2)}) copy-start(bf16[512,8,64]{2,0,1:T(8,128)(2,1)} %get-tuple-element.7) | copy-start | bytes 1572868
  110.6 12.3 %copy-start.4 = (bf16[512,8,64]{2,0,1:T(8,128)(2,1)S(1)}, bf16[512,8,64]{2,0,1:T(8,128)(2,1)}, u32[]{:S(2)}) copy-start(bf16[512,8,64]{2,0,1:T(8,128)(2,1)} %get-tuple-element.38) | copy-start | bytes 1572868
  118.6 17.4 %all-to-all-start.4 = ((bf16[128,4,1024]{0,2,1:T(8,128)(2,1)}), bf16[128,4,1024]{0,2,1:T(8,128)(2,1)}, u32[]{:S(2)}, u32[]{:S(2)}) async-start(bf16[128,4,1024]{0,2,1:T(8,128)(2,1)} %bitcast.114), calls=%async_computation.4 | async-start | bytes 2097152 | tf_op jit(solution)/shard_map/all_to_all | solution.py:134
  125.5 3.3 copy-start.1
  131.1 11.9 %copy-start.14 = (bf16[1,128,4096]{2,1,0:T(8,128)(2,1)S(1)}, bf16[1,128,4096]{2,1,0:T(8,128)(2,1)}, u32[]{:S(2)}) copy-start(bf16[1,128,4096]{2,1,0:T(8,128)(2,1)} %param.27) | copy-start | bytes 3145732
  136.1 43.1 %all-to-all-start.2 = ((bf16[128,4,1024]{0,2,1:T(8,128)(2,1)}), bf16[128,4,1024]{0,2,1:T(8,128)(2,1)}, u32[]{:S(2)}, u32[]{:S(2)}) async-start(bf16[128,4,1024]{0,2,1:T(8,128)(2,1)} %bitcast.10), calls=%async_computation.2 | async-start | bytes 2097152 | tf_op jit(solution)/shard_map/all_to_all | solution.py:132
  179.2 32.4 %all-to-all-start.5 = ((bf16[128,4,1024]{0,2,1:T(8,128)(2,1)}), bf16[128,4,1024]{0,2,1:T(8,128)(2,1)}, u32[]{:S(2)}, u32[]{:S(2)}) async-start(bf16[128,4,1024]{0,2,1:T(8,128)(2,1)} %bitcast.112), calls=%async_computation.5 | async-start | bytes 2097152 | tf_op jit(solution)/shard_map/all_to_all | solution.py:135
  190.3 5.9 %copy-start = (f32[8,512,512]{1,2,0:T(8,128)}, f32[8,512,512]{1,2,0:T(8,128)S(1)}, u32[]{:S(2)}) copy-start(f32[8,512,512]{1,2,0:T(8,128)S(1)} %fusion.48) | copy-start | bytes 25165828
  216.9 5.2 copy-start.15
  216.9 189.0 %all-to-all-start.6 = ((bf16[8,512,1024]{1,2,0:T(8,128)(2,1)}), bf16[8,512,1024]{1,2,0:T(8,128)(2,1)}, u32[]{:S(2)}, u32[]{:S(2)}) async-start(bf16[8,512,1024]{1,2,0:T(8,128)(2,1)} %broadcast_in_dim.28), calls=%async_computation.7 | async-start | bytes 16777216 | tf_op jit(solution)/shard_map/all_to_all | solution.py:176
  222.1 183.9 %reduce-scatter.2.cloned.1.call-start = ((), (), s32[]{:S(2)}) async-start(), calls=%async_computation.10 | async-start | bytes 6553600 | tf_op jit(solution)/shard_map/reduce_scatter | solution.py:177
  234.6 10.3 %copy-start.16 = (bf16[512,8,128]{0,2,1:T(8,128)(2,1)S(1)}, bf16[512,8,128]{0,2,1:T(8,128)(2,1)}, u32[]{:S(2)}) copy-start(bf16[512,8,128]{0,2,1:T(8,128)(2,1)} %reshape.307) | copy-start | bytes 3145732
  244.9 11.6 %copy-start.9 = (bf16[512,8,128]{0,2,1:T(8,128)(2,1)S(1)}, bf16[512,8,128]{0,2,1:T(8,128)(2,1)}, u32[]{:S(2)}) copy-start(bf16[512,8,128]{0,2,1:T(8,128)(2,1)} %fusion.25) | copy-start | bytes 3145732
  276.8 129.2 %copy-start.10 = (bf16[1,128,5120]{2,1,0:T(8,128)(2,1)S(1)}, bf16[1,128,5120]{2,1,0:T(8,128)(2,1)}, u32[]{:S(2)}) copy-start(bf16[1,128,5120]{2,1,0:T(8,128)(2,1)} %param.18) | copy-start | bytes 3932164
  276.8 227.4 %all-gather.5.cloned.1.call-start = ((), (), s32[]{:S(2)}) async-start(), calls=%async_computation.11 | async-start | bytes 6553600 | tf_op jit(solution)/shard_map/all_gather | solution.py:188
  407.7 108.9 %copy-start.2 = (bf16[128,5120]{1,0:T(8,128)(2,1)}, bf16[128,5120]{1,0:T(8,128)(2,1)S(1)}, u32[]{:S(2)}) copy-start(bf16[128,5120]{1,0:T(8,128)(2,1)S(1)} %fusion.21) | copy-start | bytes 3932164
Sparse Core Ops, SparseCore 0:
  10.9 188.0 all-gather.2
  276.9 63.2 reduce-scatter.1
  443.3 60.8 all-gather.4
where the time goes:
time: 533 us; the launch traced here: 524 us
  waiting for transfers between devices  200 us (38%)
  matrix products  112 us (21%)
  local copies, waits for them, and re-layouts  85.2 us (16%)
  other arithmetic  41.9 us (8%)
  blocking collectives  35.4 us (7%)
  starting transfers between devices  32.9 us (6%)
  between operations  16.1 us (3%)
    all_to_all x1, waiting for transfers between devices, local(): lax.all_to_all(copies, 'dp', split_axis=0, concat_axis=0, tiled=True)  129 us
    all_gather x1, waiting for transfers between devices, local(): columns = lax.all_gather(columns, 'tensor', axis=0, tiled=True)  61 us
    unnamed x54, local copies, waits for them, and re-layouts  40.8 us
    all_to_all x1, blocking collectives, local(): lax.all_to_all(target.reshape(seq_local, clips, width), 'dp', split_axis=...  35.4 us
    dot_general x2, matrix products, attend_plain(): jnp.einsum('hqk,khd->qhd', rounded, value_rows, preferred_element_type=jn...  21 us
    another operation x2, other arithmetic  15.4 us
    sub x3, other arithmetic, softmax_rows(): exponent = jnp.exp(scores - row_peak)  15.2 us
    dot_general x1, matrix products, local(): jnp.einsum('csi,scd->cid', attended_all, columns, preferred_element_type=...  12.3 us
  transfers between devices with their start and end apart: 10, of which 4 were waited for; matrix products, arithmetic and copies ran while one was open for 41% of the time, Pallas kernels for 0%

commit v1 on v0

--- a/solution.py
+++ b/solution.py
@@ -8,6 +8,35 @@
 STEPS = 1000
 sigma_data = 0.5
 guidance = 5.0
+
+
+def stocks_enter(xs, which_dim, s0):
+    v_next = xs.shape
+    formed = xs.reshape(*v_next[:which_dim], s0, v_next[which_dim] // s0, *v_next[which_dim + 1 :])
+    return jnp.moveaxis(formed, which_dim, 0)
+
+
+def plan_the_words(xx, axis_k):
+    parts_out = list(xx.shape[1:])
+    parts_out[axis_k] *= xx.shape[0]
+    return jnp.moveaxis(xx, 0, axis_k).reshape(parts_out)
+
+
+def place_orders(load, my_data, row_data, axis_tag):
+    value_now, piece_out = (lax.axis_size(axis_tag), lax.axis_index(axis_tag))
+    k_now = stocks_enter(my_data, load, value_now)
+    buffers = [k_now[piece_out]]
+    for dd in range(1, value_now):
+        taken_in = k_now[piece_out ^ dd]
+        buffers.append(
+            lax.ppermute(
+                taken_in,
+                axis_name=axis_tag,
+                perm=[(src_i, src_i ^ dd) for src_i in range(value_now)],
+            )
+        )
+    k_now = jnp.stack(buffers, axis=0)[piece_out ^ jnp.arange(value_now)]
+    return plan_the_words(k_now, row_data)
 
 
 def rope_angles(coords):
@@ -128,7 +157,7 @@
     )
     arrived = (
         lax.all_to_all(outgoing[0], "tensor", split_axis=1, concat_axis=0, tiled=True),
-        lax.all_to_all(outgoing[1], "tensor", split_axis=1, concat_axis=0, tiled=True),
+        place_orders(1, outgoing[1], 0, "tensor"),
         lax.all_to_all(outgoing[2], "tensor", split_axis=1, concat_axis=0, tiled=True),
         lax.all_to_all(outgoing[3], "tensor", split_axis=1, concat_axis=0, tiled=True),
         lax.all_to_all(outgoing[4], "tensor", split_axis=1, concat_axis=0, tiled=True),

time: 533 us -> 529 us (level)
  waiting for transfers between devices: 200 us -> 194 us
    sub x3, other arithmetic: 15.2 us -> 21.2 us  [softmax_rows(): exponent = jnp.exp(scores - row_peak)]
    all_to_all x1 -> x0, waiting for transfers between devices: 5.37 us -> none  [local(): lax.all_to_all(outgoing[1], 'tensor', split_axis=1, concat_axis=0, tiled=...]
    unnamed x54 -> x52, local copies, waits for them, and re-layouts: 40.8 us -> 39.1 us
    another operation x2 -> x3, other arithmetic: 15.4 us -> 14.4 us
  transfers between devices with their start and end apart: 10 -> 12, of which waited for: 4 -> 3; matrix products, arithmetic and copies ran while one was open for 41% -> 43% of each run, Pallas kernels for 0% -> 0%
where the time goes in v1:
time: 529 us; the launch traced here: 524 us
  waiting for transfers between devices  194 us (37%)
  matrix products  111 us (21%)
  local copies, waits for them, and re-layouts  87.4 us (17%)
  other arithmetic  46.7 us (9%)
  blocking collectives  35.4 us (7%)
  starting transfers between devices  33.1 us (6%)
  between operations  16.1 us (3%)
    all_to_all x1, waiting for transfers between devices, local(): lax.all_to_all(copies, 'dp', split_axis=0, concat_axis=0, tiled=True)  129 us
    all_gather x1, waiting for transfers between devices, local(): columns = lax.all_gather(columns, 'tensor', axis=0, tiled=True)  60.9 us
    unnamed x52, local copies, waits for them, and re-layouts  39.1 us
    all_to_all x1, blocking collectives, local(): lax.all_to_all(target.reshape(seq_local, clips, width), 'dp', split_axis=...  35.4 us
    dot_general x2, matrix products, attend_plain(): jnp.einsum('hqk,khd->qhd', rounded, value_rows, preferred_element_type=jn...  21.4 us
    sub x3, other arithmetic, softmax_rows(): exponent = jnp.exp(scores - row_peak)  21.2 us
    another operation x2, other arithmetic  13.2 us
    dot_general x1, matrix products, local(): jnp.einsum('csi,scd->cid', attended_all, columns, preferred_element_type=...  12.3 us
  transfers between devices with their start and end apart: 12, of which 3 were waited for; matrix products, arithmetic and copies ran while one was open for 43% of the time, Pallas kernels for 0%

profile of v1, /device:TPU:0, one launch (start us, length us, event | category | flops | bytes accessed | tf_op | source)
XLA Modules:
  0.0 524.2 jit_solution(2118055370871124230)
XLA Ops:
  7.2 3.6 pad_maximum_fusion
  11.4 2.7 copy.151
  14.1 2.6 copy.155
  16.7 1.6 copy.141
  19.8 6.3 %subtract_convert_fusion.5 = (bf16[128,32,64]{0,2,1:T(8,128)(2,1)}, bf16[128,32,64]{0,2,1:T(8,128)(2,1)}, bf16[128,32,64]{0,2,1:T(8,128)(2,1)S(1)}, bf16[128,32,...) fusion(f32[128,32,128]{0,2,1:T(8,128)} %bitcast.112, ...), kind=kLoop, calls=%fused_computation.78 | loop fusion | flops 8388608 | bytes 12648448 | tf_op jit(solution)/shard_map/convert.16
  27.7 3.0 collective-permute-start
  31.6 1.5 collective-permute-start.1
  35.0 4.6 all-to-all-start.2
  40.7 2.7 fusion.92
  43.9 1.6 fusion.97
  45.5 1.8 copy.188
  47.4 3.2 copy.189
  50.5 3.1 fusion.91
  53.6 1.5 copy.190
  55.1 1.6 fusion.96
  56.8 3.2 copy.191
  59.9 3.1 copy.192
  63.1 1.5 copy.193
  64.6 1.6 fusion.95
  66.3 3.2 copy.194
  69.5 3.2 copy.195
  72.7 1.5 copy.196
  74.2 1.6 fusion.94
  75.8 3.2 copy.197
  79.0 3.2 copy.198
  82.2 6.9 %subtract_convert_fusion = (bf16[512,8,64]{2,0,1:T(8,128)(2,1)S(1)}, bf16[512,8,64]{2,0,1:T(8,128)(2,1)S(1)}, bf16[512,8,64]{2,0,1:T(8,128)(2,1)S(1)}, bf16[512,...) fusion(f32[512,8,64]{2,0,1:T(8,128)} %copy.198, ...), kind=kLoop, calls=%fused_computation.42 | loop fusion | flops 8388608 | bytes 12845056 | tf_op jit(solution)/shard_map/convert.8
  90.3 4.6 fusion.30
  94.9 4.7 fusion.37
  99.6 4.9 all-to-all-start
  104.5 1.7 fusion.93
  107.8 2.3 copy.148
  110.1 2.3 copy.160
  114.9 2.3 pad_maximum_fusion.5
  117.2 8.0 %fusion.98 = f32[8,512]{1,0:T(8,128)S(1)} fusion(f32[8,512,512]{1,2,0:T(8,128)} %fusion.30), kind=kOutput, calls=%fused_computation.134 | output fusion | flops 8389119 | bytes 8404992 | tf_op jit(solution)/shard_map/sub | solution.py:91
  125.2 4.3 all-to-all-start.3
  129.6 8.1 %fusion.99 = f32[8,512]{1,0:T(8,128)S(1)} fusion(f32[8,512,512]{1,2,0:T(8,128)} %fusion.37), kind=kOutput, calls=%fused_computation.135 | output fusion | flops 8389119 | bytes 8404992 | tf_op jit(solution)/shard_map/sub | solution.py:91
  137.6 3.9 all-to-all-done.3
  141.5 4.4 all-to-all-start.1
  146.0 10.6 %fusion.19 = f32[8,512,128]{1,2,0:T(8,128)} fusion(bf16[512,8,128]{0,2,1:T(8,128)(2,1)} %bitcast.134, f32[8,512]{1,0:T(8,128)S(1)} %fusion.98, f32[8,512,512]{1,2,0:T(8,128)} %fusion.30), kind=kOutput, calls=%fused_computation.31 | convolution fusion | flops 547361280 | bytes 11550720 | tf_op jit(solution)/shard_map/hqk,khd->qhd/dot_general | solution.py:100
  156.5 10.8 %fusion.25 = bf16[512,8,128]{0,2,1:T(8,128)(2,1)} fusion(f32[8,512,128]{1,2,0:T(8,128)} %fusion.19, f32[]{:T(128)} %bitcast.33, pred[]{:T(512)} %bitcast.34, bf16[512,8,128]{0,2,1:T(8,128)(2,1)S(1)} %bitcast.132, f32[8,512]{1,0:T(8,128)S(1)} %fusion.99, f32[8,512,512]{1,2,0:T(8,128)} %fusion.37), kind=kOutput, calls=%fused_computation.40 | convolution fusion | flops 551031296 | bytes 12599301 | tf_op jit(solution)/shard_map/hqk,khd->qhd/dot_general | solution.py:100
  169.5 1.5 copy.152
  171.3 2.3 copy.140
  173.6 1.5 copy.200
  175.1 2.3 copy.156
  177.3 2.5 copy.203
  179.9 4.5 all-to-all-start.4
  184.3 3.0 copy.149
  187.3 2.2 reshape.320
  190.8 5.1 fusion.100
  196.7 10.9 %fusion.101 = (bf16[8,512,128]{1,2,0:T(8,128)(2,1)}, f32[8,512,128]{1,2,0:T(8,128)}) fusion(bf16[512,8,128]{0,2,1:T(8,128)(2,1)} %reshape.320, f32[8,512]{1,0:T(8,128)S(1)} %get-tuple-element.60, f32[8,512,512]{1,2,0:T(8,128)} %copy-done), kind=kOutput, calls=%fused_computation.137 | convolution fusion | flops 547885568 | bytes 12599296 | tf_op jit(solution)/shard_map/hqk,khd->qhd/dot_general | solution.py:111
  207.6 4.4 fusion.45
  212.1 5.1 broadcast_in_dim.28
  217.2 5.5 %all-to-all-start.5 = ((bf16[8,512,1024]{1,2,0:T(8,128)(2,1)}), bf16[8,512,1024]{1,2,0:T(8,128)(2,1)}, u32[]{:S(2)}, u32[]{:S(2)}) async-start(bf16[8,512,1024]{1,2,0:T(8,128)(2,1)} %broadcast_in_dim.28), calls=%async_computation.6 | async-start | bytes 16777216 | tf_op jit(solution)/shard_map/all_to_all | solution.py:205
  222.7 10.0 %multiply_reduce_fusion = (f32[8,512]{1,0:T(8,128)S(1)}, f32[8,512,512]{1,2,0:T(8,128)}) fusion(f32[8,512,512]{1,2,0:T(8,128)} %get-tuple-element.61, f32[8,512]{1,0:T(8,128)S(1)} %get-tuple-element.60, f32[8,512,512]{1,2,0:T(8,128)} %fusion.45, bf16[512,8,128]{2,1,0:T(8,128)(2,1)S(1)} %bitcast.133, bf16[512,8,128]{2,1,0:T(8,128)(2,1)S(1)} %bitcast.118), kind=kOutput, calls=%fused_computation.16 | convolution fusion | flops 547352576 | bytes 27295744 | tf_op jit(solution)/shard_map/qhd,khd->hqk/dot_general | solution.py:114
  232.7 2.0 copy.161
  235.2 10.2 %fusion.28 = f32[8,512,128]{1,2,0:T(8,128)} fusion(bf16[512,8,128]{0,2,1:T(8,128)(2,1)S(1)} %reshape.323, f32[8,512]{1,0:T(8,128)S(1)} %get-tuple-element.60, f32[8,512,512]{1,2,0:T(8,128)} %copy-done), kind=kOutput, calls=%fused_computation.52 | convolution fusion | flops 547361280 | bytes 11550720 | tf_op jit(solution)/shard_map/hqk,khd->qhd/dot_general | solution.py:120
  245.4 11.3 %subtract_convert_fusion.4 = bf16[8,512,128]{1,2,0:T(8,128)(2,1)S(1)} fusion(f32[8,512,128]{1,2,0:T(8,128)} %fusion.28, f32[8,512,128]{1,2,0:T(8,128)} %get-tuple-element.65, bf16[512,8,128]{0,2,1:T(8,128)(2,1)S(1)} %copy-done.13, f32[8,512,512]{1,2,0:T(8,128)} %get-tuple-element.63, f32[8,512]{1,0:T(8,128)S(1)} %get-tuple-element.62, f32[]{:T(128)S(6)} %mul.409, ...), kind=kOutput, calls=%fused_computation.49 | convolution fusion | flops 554177024 | bytes 23101448 | tf_op jit(solution)/shard_map/hqk,khd->qhd/dot_general | solution.py:118
  256.7 8.4 %fusion.3 = f32[512,5120]{1,0:T(8,128)S(1)} fusion(bf16[512,1024]{0,1:T(8,128)(2,1)S(1)} %bitcast.128, bf16[2,1024,5120]{2,1,0:T(8,128)(2,1)} %all-gather.3.cloned.1.call-done), kind=kOutput, calls=%fused_computation.7 | convolution fusion | flops 5368709120 | bytes 22020096 | tf_op jit(solution)/shard_map/dot_general | solution.py:199
  265.1 11.9 %add_convert_fusion = bf16[512,5120]{1,0:T(8,128)(2,1)} fusion(f32[512,5120]{1,0:T(8,128)S(1)} %fusion.3, bf16[512,1024]{0,1:T(8,128)(2,1)S(1)} %bitcast.136, bf16[2,1024,5120]{2,1,0:T(8,128)(2,1)} %all-gather.3.cloned.1.call-done), kind=kOutput, calls=%fused_computation.10 | convolution fusion | flops 5373952000 | bytes 27262976 | tf_op jit(solution)/shard_map/dot_general | solution.py:199
  277.4 129.2 %all-to-all-done.5 = bf16[8,512,1024]{1,2,0:T(8,128)(2,1)} async-done(((bf16[8,512,1024]{1,2,0:T(8,128)(2,1)}), bf16[8,512,1024]{1,2,0:T(8,128)(2,1)}, u32[]{:S(2)}, u32[]{:S(2)}) %all-to-all-start.5) | async-done | bytes 8388640 | tf_op jit(solution)/shard_map/all_to_all | solution.py:205
  406.7 1.7 fusion.21
  408.5 35.4 %all_to_all.81 = bf16[128,8,640]{2,0,1:T(8,128)(2,1)} all-to-all(bf16[128,8,640]{2,0,1:T(8,128)(2,1)S(1)} %bitcast.116), channel_id=1, replica_groups=mesh['dp'=8,'tensor'=4] {'dp'}, dimensions={1} | all-to-all | bytes 2621440 | tf_op jit(solution)/shard_map/all_to_all | solution.py:214
  443.9 60.9 %all-gather.5.cloned.1.call-done = bf16[512,8,640]{2,0,1:T(8,128)(2,1)} async-done(((bf16[128,8,640]{2,0,1:T(8,128)(2,1)}), bf16[512,8,640]{2,0,1:T(8,128)(2,1)}) %all-gather.5.cloned.1.call-update) | async-done | bytes 5242896 | tf_op jit(solution)/shard_map/all_gather | solution.py:217
  504.8 12.3 %convert_reduce_fusion = f32[1024,640]{1,0:T(8,128)} fusion(bf16[8,512,1024]{1,2,0:T(8,128)(2,1)} %all-to-all-done.5, bf16[512,8,640]{2,0,1:T(8,128)(2,1)} %all-gather.5.cloned.1.call-done), kind=kOutput, calls=%fused_computation.4 | convolution fusion | flops 5389025280 | bytes 16252928 | tf_op jit(solution)/shard_map/csi,scd->cid/dot_general | solution.py:219
  (78 shorter events, 17.3 us)
Async XLA Ops:
  7.2 3.6 copy-start.9
  7.2 249.5 %all-gather.3.cloned.1.call-start = ((), (), s32[]{:S(2)}) async-start(), calls=%async_computation.8 | async-start | bytes 23592960 | tf_op jit(solution)/shard_map/all_gather | solution.py:198
  11.4 5.4 %copy-start.10 = (bf16[1,128,4096]{2,1,0:T(8,128)(2,1)S(1)}, bf16[1,128,4096]{2,1,0:T(8,128)(2,1)}, u32[]{:S(2)}) copy-start(bf16[1,128,4096]{2,1,0:T(8,128)(2,1)} %param.23) | copy-start | bytes 3145732
  11.4 7.0 %copy-start.16 = (s32[1,3,512]{2,0,1:T(1,128)S(1)}, s32[1,3,512]{2,0,1:T(1,128)}, u32[]{:S(2)}) copy-start(s32[1,3,512]{2,0,1:T(1,128)} %param.17) | copy-start | bytes 18436
  26.0 13.6 %copy-start.15 = (f32[512,64]{0,1:T(8,128)S(1)}, f32[512,64]{0,1:T(8,128)}, u32[]{:S(2)}) copy-start(f32[512,64]{0,1:T(8,128)} %get-tuple-element.55) | copy-start | bytes 393220
  27.7 139.6 %collective-permute-start = (bf16[128,1024]{1,0:T(8,128)(2,1)}, bf16[128,1024]{1,0:T(8,128)(2,1)}, u32[]{:S(2)}, u32[]{:S(2)}) collective-permute-start(bf16[128,1024]{1,0:T(8,128)(2,1)} %bitcast.10), channel_id=1, source_target_pairs={{0,1},{1,0},{2,3},{3,2},{4,5},{5,4},{6,7},{7,6},{8,9},{9,8},{10,11... | collective-permute-start | bytes 786440 | tf_op jit(solution)/shard_map/ppermute | solution.py:32
  31.6 135.8 %collective-permute-start.1 = (bf16[128,1024]{1,0:T(8,128)(2,1)}, bf16[128,1024]{1,0:T(8,128)(2,1)}, u32[]{:S(2)}, u32[]{:S(2)}) collective-permute-start(bf16[128,1024]{1,0:T(8,128)(2,1)} %bitcast.12), channel_id=1, source_target_pairs={{0,2},{1,3},{2,0},{3,1},{4,6},{5,7},{6,4},{7,5},{8,10},{9,11},{10,... | collective-permute-start | bytes 786440 | tf_op jit(solution)/shard_map/ppermute | solution.py:32
  34.0 133.4 %collective-permute-start.2 = (bf16[128,1024]{1,0:T(8,128)(2,1)}, bf16[128,1024]{1,0:T(8,128)(2,1)}, u32[]{:S(2)}, u32[]{:S(2)}) collective-permute-start(bf16[128,1024]{1,0:T(8,128)(2,1)} %bitcast.14), channel_id=1, source_target_pairs={{0,3},{1,2},{2,1},{3,0},{4,7},{5,6},{6,5},{7,4},{8,11},{9,10},{10,... | collective-permute-start | bytes 786440 | tf_op jit(solution)/shard_map/ppermute | solution.py:32
  35.0 64.5 %all-to-all-start.2 = ((bf16[128,4,1024]{0,2,1:T(8,128)(2,1)}), bf16[128,4,1024]{0,2,1:T(8,128)(2,1)}, u32[]{:S(2)}, u32[]{:S(2)}) async-start(bf16[128,4,1024]{0,2,1:T(8,128)(2,1)} %bitcast.21), calls=%async_computation.2 | async-start | bytes 2097152 | tf_op jit(solution)/shard_map/all_to_all | solution.py:162
  75.8 6.4 %copy-start.8 = (f32[512,64]{1,0:T(8,128)S(1)}, f32[512,64]{1,0:T(8,128)}, u32[]{:S(2)}) copy-start(f32[512,64]{1,0:T(8,128)} %copy.167) | copy-start | bytes 393220
  82.2 7.0 %copy-start.4 = (bf16[128,32,64]{0,2,1:T(8,128)(2,1)S(1)}, bf16[128,32,64]{0,2,1:T(8,128)(2,1)}, u32[]{:S(2)}) copy-start(bf16[128,32,64]{0,2,1:T(8,128)(2,1)} %get-tuple-element.52) | copy-start | bytes 1572868
  82.2 7.0 %copy-start.5 = (bf16[128,32,64]{0,2,1:T(8,128)(2,1)S(1)}, bf16[128,32,64]{0,2,1:T(8,128)(2,1)}, u32[]{:S(2)}) copy-start(bf16[128,32,64]{0,2,1:T(8,128)(2,1)} %get-tuple-element.53) | copy-start | bytes 1572868
  99.6 7.4 %copy-start.11 = (bf16[128,1,1024]{0,2,1:T(8,128)(2,1)S(1)}, bf16[128,1,1024]{0,2,1:T(8,128)(2,1)}, u32[]{:S(2)}) copy-start(bf16[128,1,1024]{0,2,1:T(8,128)(2,1)} %get-tuple-element.28) | copy-start | bytes 786436
  99.6 25.7 %all-to-all-start = ((bf16[128,4,1024]{0,2,1:T(8,128)(2,1)}), bf16[128,4,1024]{0,2,1:T(8,128)(2,1)S(1)}, u32[]{:S(2)}, u32[]{:S(2)}) async-start(bf16[128,4,1024]{0,2,1:T(8,128)(2,1)} %bitcast.5), calls=%async_computation | async-start | bytes 2097152 | tf_op jit(solution)/shard_map/all_to_all | solution.py:159
  125.2 12.4 %copy-start.2 = (bf16[128,4,1024]{0,2,1:T(8,128)(2,1)}, bf16[128,4,1024]{0,2,1:T(8,128)(2,1)S(1)}, u32[]{:S(2)}) copy-start(bf16[128,4,1024]{0,2,1:T(8,128)(2,1)S(1)} %all-to-all-done) | copy-start | bytes 3145732
  125.2 16.3 %all-to-all-start.3 = ((bf16[128,4,1024]{0,2,1:T(8,128)(2,1)}), bf16[128,4,1024]{0,2,1:T(8,128)(2,1)S(1)}, u32[]{:S(2)}, u32[]{:S(2)}) async-start(bf16[128,4,1024]{0,2,1:T(8,128)(2,1)} %bitcast.24), calls=%async_computation.3 | async-start | bytes 2097152 | tf_op jit(solution)/shard_map/all_to_all | solution.py:163
  141.5 15.0 %copy-start.3 = (bf16[128,4,1024]{0,2,1:T(8,128)(2,1)}, bf16[128,4,1024]{0,2,1:T(8,128)(2,1)S(1)}, u32[]{:S(2)}) copy-start(bf16[128,4,1024]{0,2,1:T(8,128)(2,1)S(1)} %all-to-all-done.3) | copy-start | bytes 3145732
  141.5 38.3 %all-to-all-start.1 = ((bf16[128,4,1024]{0,2,1:T(8,128)(2,1)}), bf16[128,4,1024]{0,2,1:T(8,128)(2,1)}, u32[]{:S(2)}, u32[]{:S(2)}) async-start(bf16[128,4,1024]{0,2,1:T(8,128)(2,1)} %bitcast.17), calls=%async_computation.1 | async-start | bytes 2097152 | tf_op jit(solution)/shard_map/all_to_all | solution.py:161
  156.5 10.8 %copy-start.14 = (bf16[128,1,1024]{2,0,1:T(8,128)(2,1)S(1)}, bf16[128,1,1024]{2,0,1:T(8,128)(2,1)}, u32[]{:S(2)}) copy-start(bf16[128,1,1024]{2,0,1:T(8,128)(2,1)} %copy.142) | copy-start | bytes 786436
  179.9 32.2 %all-to-all-start.4 = ((bf16[128,4,1024]{0,2,1:T(8,128)(2,1)}), bf16[128,4,1024]{0,2,1:T(8,128)(2,1)}, u32[]{:S(2)}, u32[]{:S(2)}) async-start(bf16[128,4,1024]{0,2,1:T(8,128)(2,1)} %bitcast.122), calls=%async_computation.4 | async-start | bytes 2097152 | tf_op jit(solution)/shard_map/all_to_all | solution.py:164
  190.8 5.9 %copy-start = (f32[8,512,512]{1,2,0:T(8,128)}, f32[8,512,512]{1,2,0:T(8,128)S(1)}, u32[]{:S(2)}) copy-start(f32[8,512,512]{1,2,0:T(8,128)S(1)} %fusion.48) | copy-start | bytes 25165828
  217.2 5.5 %copy-start.12 = (bf16[64,8,8,128]{3,2,1,0:T(8,128)(2,1)S(1)}, bf16[64,8,8,128]{3,2,1,0:T(8,128)(2,1)}, u32[]{:S(2)}) copy-start(bf16[64,8,8,128]{3,2,1,0:T(8,128)(2,1)} %copy.203) | copy-start | bytes 3145732
  217.2 189.5 %all-to-all-start.5 = ((bf16[8,512,1024]{1,2,0:T(8,128)(2,1)}), bf16[8,512,1024]{1,2,0:T(8,128)(2,1)}, u32[]{:S(2)}, u32[]{:S(2)}) async-start(bf16[8,512,1024]{1,2,0:T(8,128)(2,1)} %broadcast_in_dim.28), calls=%async_computation.6 | async-start | bytes 16777216 | tf_op jit(solution)/shard_map/all_to_all | solution.py:205
  222.7 184.0 %reduce-scatter.2.cloned.1.call-start = ((), (), s32[]{:S(2)}) async-start(), calls=%async_computation.9 | async-start | bytes 6553600 | tf_op jit(solution)/shard_map/reduce_scatter | solution.py:206
  235.2 10.2 %copy-start.13 = (bf16[512,8,128]{0,2,1:T(8,128)(2,1)S(1)}, bf16[512,8,128]{0,2,1:T(8,128)(2,1)}, u32[]{:S(2)}) copy-start(bf16[512,8,128]{0,2,1:T(8,128)(2,1)} %reshape.320) | copy-start | bytes 3145732
  245.4 11.3 %copy-start.6 = (bf16[512,8,128]{0,2,1:T(8,128)(2,1)S(1)}, bf16[512,8,128]{0,2,1:T(8,128)(2,1)}, u32[]{:S(2)}) copy-start(bf16[512,8,128]{0,2,1:T(8,128)(2,1)} %fusion.25) | copy-start | bytes 3145732
  277.1 129.6 %copy-start.7 = (bf16[1,128,5120]{2,1,0:T(8,128)(2,1)S(1)}, bf16[1,128,5120]{2,1,0:T(8,128)(2,1)}, u32[]{:S(2)}) copy-start(bf16[1,128,5120]{2,1,0:T(8,128)(2,1)} %param.18) | copy-start | bytes 3932164
  277.1 227.7 %all-gather.5.cloned.1.call-start = ((), (), s32[]{:S(2)}) async-start(), calls=%async_computation.10 | async-start | bytes 6553600 | tf_op jit(solution)/shard_map/all_gather | solution.py:217
  408.4 108.8 %copy-start.1 = (bf16[128,5120]{1,0:T(8,128)(2,1)}, bf16[128,5120]{1,0:T(8,128)(2,1)S(1)}, u32[]{:S(2)}) copy-start(bf16[128,5120]{1,0:T(8,128)(2,1)S(1)} %fusion.21) | copy-start | bytes 3932164
Sparse Core Ops, SparseCore 0:
  10.9 188.0 all-gather.2
  277.2 63.3 reduce-scatter.1
  444.0 60.7 all-gather.4
